TPU v7x, 512 devices: a whole 4x8x8 slice. The times are simulated.
512 devices in a mesh: kv: 16 (over z, core), ep: 32 (over x, y).
Axes of the slice: x: 4, y: 8, z: 8, core: 2. Of those that a mesh axis runs over, the one named last changes fastest.
Arguments:
- queries: bfloat16 [32, 64, 2048], P('ep'), may hold values from -12 to 12
- new_keys: bfloat16 [32, 64, 512], P('ep'), may hold values from -12 to 12
- new_values: bfloat16 [32, 64, 512], P('ep'), may hold values from -6 to 6
- cache_keys: bfloat16 [32, 64, 128, 512], P('ep', 'kv'), may hold values from -12 to 12
- cache_values: bfloat16 [32, 64, 128, 512], P('ep', 'kv'), may hold values from -10 to 10
- page_table: int32 [32, 64], P('ep'), may hold values from 0 to 63, each once within a row
- cached_len: int32 [32], P('ep'), may hold values from 1 to 8192, 65536 in all
- moe_rows: bfloat16 [1024, 4096], P('ep'), may hold values from -6 to 6
- expert_ids: int32 [1024, 2], P('ep'), may hold values from 0 to 7, all different within a row; in each aligned block of 32 rows (0 to 31, 32 to 63, ...) at most 16 rows name the same one
- gate_probs: float32 [1024, 2], P('ep'), may hold values from 0.1 to 0.9
- w_gate: bfloat16 [32, 4096, 2048], P('ep', None, 'kv'), may hold values from -0.09375 to 0.09375
- w_up: bfloat16 [32, 4096, 2048], P('ep', None, 'kv'), may hold values from -0.09375 to 0.09375
- w_down: bfloat16 [32, 2048, 4096], P('ep', 'kv'), may hold values from -0.09375 to 0.09375
Outputs:
- attn_out: bfloat16 [32, 64, 2048], P('ep')
- moe_out: bfloat16 [1024, 4096], P('ep', 'kv')
Inputs may be any that keep to these rules, and one draw needn't show every extreme that they name: `page_table`: each row is a permutation of the 64 slots of its request. `cached_len`: cached positions at or past a request's length hold no data. `expert_ids`: each row names 2 different experts; among the 32 rows of one ep index no expert is named more than 16 times, and this bound is reached.
All inputs are finite; a program needn't handle non-finite values. No bound on the sum of `cached_len` on one device may be relied on, other than what follows from the above.
Results may differ from a plain program's by a relative error of at most 0.0085.
Values may be sent and summed in bfloat16 or wider, within the bound.
No kernel may reach another device: no remote copies, remote signals or barrier semaphores. Data moves between devices by JAX's collectives and lax.ppermute only.
A program may use at most 128 MiB of HBM per device.

v0:
```python
import math
import jax
import jax.numpy as jnp
from jax import lax
from jax.sharding import PartitionSpec as P

HD = 128
EXPERTS = 8
TOP = 2
HQ = 16
KVH = 4
PAGE = 128
POOL_DEV = 4
CAP = 16
ROPE_BASE = 10000.0
MASKED = -1e30


def rotary(values, positions):
    half_width = values.shape[-1] // 2
    indices = jnp.arange(half_width, dtype=jnp.float32)
    frequency = jnp.power(ROPE_BASE, -2.0 * indices / values.shape[-1])
    angles = positions.astype(jnp.float32)[:, None] * frequency[None, :]
    cosine = jnp.cos(angles)[:, None, :]
    sine_part = jnp.sin(angles)[:, None, :]
    lower_half = values[..., :half_width]
    upper_half = values[..., half_width:]
    return jnp.concatenate(
        [
            lower_half * cosine - upper_half * sine_part,
            upper_half * cosine + lower_half * sine_part,
        ],
        axis=-1,
    )


def on_device(
    queries,
    new_keys,
    new_values,
    cache_keys,
    cache_values,
    page_table,
    cached_len,
    moe_rows,
    expert_ids,
    gate_probs,
    w_gate,
    w_up,
    w_down,
):
    kv_index = lax.axis_index("kv")
    kv_count = lax.axis_size("kv")
    all_rows = queries.shape[1]
    block_rows = all_rows // kv_count
    length = cached_len[0]
    group_size = HQ // KVH
    score_scale = 1.0 / math.sqrt(HD)
    slot_ids = kv_index * POOL_DEV + jnp.arange(POOL_DEV, dtype=jnp.int32)
    matches = (page_table[0][:, None] == slot_ids[None, :]).astype(jnp.int32)
    page_index = jnp.sum(
        matches * jnp.arange(page_table.shape[1], dtype=jnp.int32)[:, None], axis=0
    )
    cached_pos = (page_index[:, None] * PAGE + jnp.arange(PAGE, dtype=jnp.int32)[None, :]).reshape(
        -1
    )
    block_start = kv_index * block_rows
    own_pos = length + block_start + jnp.arange(block_rows, dtype=jnp.int32)
    key_block = lax.dynamic_slice_in_dim(new_keys[0], block_start, block_rows, 0)
    value_block = lax.dynamic_slice_in_dim(new_values[0], block_start, block_rows, 0)
    own_keys = rotary(key_block.astype(jnp.float32).reshape(block_rows, KVH, HD), own_pos).astype(
        jnp.bfloat16
    )
    local_keys = jnp.concatenate([cache_keys[0].reshape(-1, KVH, HD), own_keys], axis=0)
    local_values = jnp.concatenate(
        [cache_values[0].reshape(-1, KVH, HD), value_block.reshape(block_rows, KVH, HD)], axis=0
    )
    key_pos = jnp.concatenate([cached_pos, own_pos])
    live_keys = jnp.concatenate([cached_pos < length, jnp.ones((block_rows,), jnp.bool_)])
    positions = length + jnp.arange(all_rows, dtype=jnp.int32)
    rotated = rotary(queries[0].astype(jnp.float32).reshape(all_rows, HQ, HD), positions).astype(
        jnp.bfloat16
    )
    grouped = rotated.reshape(all_rows, KVH, group_size, HD)
    scores = (
        jnp.einsum("nkgd,mkd->nkgm", grouped, local_keys, preferred_element_type=jnp.float32)
        * score_scale
    )
    usable = (live_keys[None, :] & (key_pos[None, :] <= positions[:, None]))[:, None, None, :]
    scores = jnp.where(usable, scores, MASKED)
    part_high = jnp.max(scores, axis=-1)
    highest = lax.pmax(part_high, "kv")
    weights = jnp.where(usable, jnp.exp(scores - highest[..., None]), 0.0)
    part_total = jnp.sum(weights, axis=-1)
    part_blend = jnp.einsum(
        "nkgm,mkd->nkgd",
        weights.astype(jnp.bfloat16),
        local_values,
        preferred_element_type=jnp.float32,
    )
    total_row = jnp.pad(part_total.reshape(1, -1), ((0, 0), (0, HQ * HD - all_rows * HQ)))
    packed = lax.psum(
        jnp.concatenate([part_blend.reshape(all_rows, HQ * HD), total_row], axis=0), "kv"
    )
    row_total = packed[all_rows, : all_rows * HQ].reshape(all_rows, HQ)
    blended = packed[:all_rows].reshape(all_rows, HQ, HD)
    attn_out = (blended / row_total[..., None]).reshape(1, all_rows, HQ * HD).astype(jnp.bfloat16)
    ep_count = lax.axis_size("ep")
    share_count = ep_count // EXPERTS
    tok_rows = moe_rows.shape[0]
    slot_total = ep_count * CAP
    flat_ids = expert_ids.reshape(-1)
    one_hot = (flat_ids[:, None] == jnp.arange(EXPERTS, dtype=jnp.int32)[None, :]).astype(jnp.int32)
    earlier = jnp.cumsum(one_hot, axis=0) - one_hot
    slot_rank = jnp.sum(earlier * one_hot, axis=1)
    slot_index = jnp.arange(slot_total, dtype=jnp.int32)
    dest_expert = slot_index // CAP // share_count
    dest_slot = slot_index % CAP
    matched = (flat_ids[None, :] == dest_expert[:, None]) & (
        slot_rank[None, :] == dest_slot[:, None]
    )
    select = jnp.sum(matched.astype(jnp.float32).reshape(slot_total, tok_rows, TOP), axis=2).astype(
        jnp.bfloat16
    )
    weight_map = jnp.sum(
        jnp.where(matched, gate_probs.reshape(-1)[None, :], 0.0).reshape(slot_total, tok_rows, TOP),
        axis=2,
    )
    col_width = moe_rows.shape[1] // kv_count
    rows_cols = lax.dynamic_slice_in_dim(moe_rows, kv_index * col_width, col_width, 1)
    outgoing = (
        jnp.dot(select, rows_cols, preferred_element_type=jnp.float32)
        .astype(jnp.bfloat16)
        .reshape(ep_count, CAP, -1)
    )
    arrived_cols = lax.all_to_all(outgoing, "ep", split_axis=0, concat_axis=0, tiled=True).reshape(
        slot_total, -1
    )
    arrived = lax.all_gather(arrived_cols, "kv", axis=1, tiled=True)
    gate_proj = jnp.dot(arrived, w_gate[0], preferred_element_type=jnp.float32)
    up_proj = jnp.dot(arrived, w_up[0], preferred_element_type=jnp.float32)
    hidden = (jax.nn.silu(gate_proj) * up_proj).astype(jnp.bfloat16)
    out_width = w_down.shape[2] // kv_count
    down_split = w_down[0].reshape(w_down.shape[1], kv_count, out_width)
    down_cols = lax.all_to_all(down_split, "kv", split_axis=1, concat_axis=0, tiled=True).reshape(
        -1, out_width
    )
    summed = jnp.dot(
        lax.all_gather(hidden, "kv", axis=1, tiled=True),
        down_cols,
        preferred_element_type=jnp.float32,
    )
    returned = (
        lax.all_to_all(
            summed.reshape(ep_count, CAP, -1).astype(jnp.bfloat16),
            "ep",
            split_axis=0,
            concat_axis=0,
            tiled=True,
        )
        .astype(jnp.float32)
        .reshape(slot_total, -1)
    )
    moe_out = jnp.dot(
        weight_map.T, returned, precision=lax.Precision.HIGHEST, preferred_element_type=jnp.float32
    ).astype(jnp.bfloat16)
    return (attn_out, moe_out)


def solution(mesh):
    return jax.shard_map(
        on_device,
        mesh=mesh,
        in_specs=(
            P("ep", None, None),
            P("ep", None, None),
            P("ep", None, None),
            P("ep", "kv", None, None),
            P("ep", "kv", None, None),
            P("ep", None),
            P("ep"),
            P("ep", None),
            P("ep", None),
            P("ep", None),
            P("ep", None, "kv"),
            P("ep", None, "kv"),
            P("ep", "kv", None),
        ),
        out_specs=(P("ep", None, None), P("ep", "kv")),
        check_vma=False,
    )
```

profile of v0, /device:TPU:2, one launch (start us, length us, event | category | flops | bytes accessed | tf_op | source)
XLA Modules:
  0.0 277.6 jit_solution(767339811898479776)
XLA Ops:
  7.2 0.8 copy.46
  8.7 0.8 convert_reduce_fusion
  9.6 1.0 convolution_convert_fusion
  10.5 21.4 %all_to_all.25 = bf16[32,16,256]{2,1,0:T(8,128)(2,1)} all-to-all(bf16[32,16,256]{2,1,0:T(8,128)(2,1)S(1)} %bitcast.94), channel_id=1, replica_groups=mesh['kv'=16,'ep'=32] {'ep'}, dimensions={0} | all-to-all | bytes 524288 | tf_op jit(solution)/shard_map/all_to_all | solution.py:136
  32.0 1.5 copy.55
  33.5 1.3 copy.48
  34.8 10.5 %all-to-all-start.1 = ((bf16[128,16,256]{2,0,1:T(8,128)(2,1)}), bf16[128,16,256]{2,0,1:T(8,128)(2,1)S(1)}, u32[]{:S(2)}, u32[]{:S(2)}) async-start(bf16[128,16,256]{2,0,1:T(8,128)(2,1)} %copy.48), calls=%async_computation.1 | async-start | bytes 2097152 | tf_op jit(solution)/shard_map/all_to_all | solution.py:145
  46.2 1.2 reshape_squeeze.10
  47.4 0.9 copy.41
  48.5 55.1 %all-gather.3.cloned.1.call-done = bf16[512,4096]{1,0:T(8,128)(2,1)} async-done(((bf16[512,256]{1,0:T(8,128)(2,1)}), bf16[512,4096]{1,0:T(8,128)(2,1)}) %all-gather.3.cloned.1.call-update) | async-done | bytes 4194320 | tf_op jit(solution)/shard_map/all_gather | solution.py:139
  103.5 3.6 %fusion.11 = f32[512,128]{1,0:T(8,128)S(1)} fusion(bf16[512,4096]{1,0:T(8,128)(2,1)} %all-gather.3.cloned.1.call-done, bf16[1,4096,128]{2,1,0:T(8,128)(2,1)S(1)} %copy-done), kind=kOutput, calls=%fused_computation.14 | convolution fusion | flops 536870912 | bytes 5505024 | tf_op jit(solution)/shard_map/dot_general | solution.py:140
  107.3 1.9 fusion.9
  111.2 2.2 fusion
  113.5 24.3 %pmax.7 = f32[64,4,4]{0,2,1:T(4,128)S(1)} all-reduce(f32[64,4,4]{0,2,1:T(4,128)S(1)} %get-tuple-element.14), channel_id=1, replica_groups=mesh['kv'=16,'ep'=32] {'kv'}, use_global_device_ids=true, to_apply=%region_2.3 | all-reduce | flops 1024 | bytes 8192 | tf_op jit(solution)/shard_map/pmax | solution.py:92
  137.8 2.6 fusion.1
  141.6 2.5 fusion.6
  144.7 0.9 select_maximum_fusion
  145.6 3.0 %all-gather.5.cloned.1.call-done = bf16[512,2048]{1,0:T(8,128)(2,1)} async-done(((bf16[512,128]{1,0:T(8,128)(2,1)}), bf16[512,2048]{1,0:T(8,128)(2,1)}) %all-gather.5.cloned.1.call-update) | async-done | bytes 2097168 | tf_op jit(solution)/shard_map/all_gather | solution.py:149
  148.6 3.0 %convolution_convert_fusion.1 = bf16[32,16,256]{2,1,0:T(8,128)(2,1)} fusion(bf16[32,16,2048]{2,1,0:T(8,128)(2,1)} %bitcast.97, bf16[2048,256,1]{1,0,2:T(8,128)(2,1)S(1)} %bitcast.91), kind=kOutput, calls=%fused_computation.9 | convolution fusion | flops 537001984 | bytes 3407872 | tf_op jit(solution)/shard_map/dot_general | solution.py:148
  151.6 9.9 %all-to-all-start.2 = ((bf16[32,16,256]{2,1,0:T(8,128)(2,1)}), bf16[32,16,256]{2,1,0:T(8,128)(2,1)S(1)}, u32[]{:S(2)}, u32[]{:S(2)}) async-start(bf16[32,16,256]{2,1,0:T(8,128)(2,1)} %convolution_convert_fusion.1), calls=%async_computation.2 | async-start | bytes 524288 | tf_op jit(solution)/shard_map/all_to_all | solution.py:154
  161.5 105.7 %all-reduce.4.cloned.1.call-done = f32[65,2048]{1,0:T(8,128)} async-done(((f32[65,2048]{1,0:T(8,128)}), f32[65,2048]{1,0:T(8,128)}) %all-reduce.4.cloned.1.call-update) | async-done | bytes 532496 | tf_op jit(solution)/shard_map/psum | solution.py:102
  267.2 0.8 slice_reduce_fusion
  268.2 1.9 fusion.24
  270.2 0.9 convolution_convert_fusion.2
  (57 shorter events, 5.3 us)
Async XLA Ops:
  7.2 96.4 %copy-start = (bf16[1,4096,128]{2,1,0:T(8,128)(2,1)S(1)}, bf16[1,4096,128]{2,1,0:T(8,128)(2,1)}, u32[]{:S(2)}) copy-start(bf16[1,4096,128]{2,1,0:T(8,128)(2,1)} %param.23) | copy-start | bytes 3145732
  7.2 96.3 %all-gather.3.cloned.1.call-start = ((), (), s32[]{:S(2)}) async-start(), calls=%async_computation.4 | async-start | bytes 4456448 | tf_op jit(solution)/shard_map/all_gather | solution.py:139
  33.5 12.6 %copy-start.4 = (bf16[1,64,2048]{2,1,0:T(8,128)(2,1)S(1)}, bf16[1,64,2048]{2,1,0:T(8,128)(2,1)}, u32[]{:S(2)}) copy-start(bf16[1,64,2048]{2,1,0:T(8,128)(2,1)} %param.13) | copy-start | bytes 786436
  34.8 13.5 %copy-start.6 = (s32[1,64]{1,0:T(1,128)S(1)}, s32[1,64]{1,0:T(1,128)}, u32[]{:S(2)}) copy-start(s32[1,64]{1,0:T(1,128)} %param.18) | copy-start | bytes 772
  34.8 110.8 %all-to-all-start.1 = ((bf16[128,16,256]{2,0,1:T(8,128)(2,1)}), bf16[128,16,256]{2,0,1:T(8,128)(2,1)S(1)}, u32[]{:S(2)}, u32[]{:S(2)}) async-start(bf16[128,16,256]{2,0,1:T(8,128)(2,1)} %copy.48), calls=%async_computation.1 | async-start | bytes 2097152 | tf_op jit(solution)/shard_map/all_to_all | solution.py:145
  45.4 103.2 %all-gather.5.cloned.1.call-start = ((), (), s32[]{:S(2)}) async-start(), calls=%async_computation.5 | async-start | bytes 2228224 | tf_op jit(solution)/shard_map/all_gather | solution.py:149
  103.5 3.6 %copy-start.1 = (bf16[512,4096]{1,0:T(8,128)(2,1)S(1)}, bf16[512,4096]{1,0:T(8,128)(2,1)}, u32[]{:S(2)}) copy-start(bf16[512,4096]{1,0:T(8,128)(2,1)} %all-gather.3.cloned.1.call-done) | copy-start | bytes 12582916
  103.5 3.7 %copy-start.5 = (bf16[1,4096,128]{2,1,0:T(8,128)(2,1)S(1)}, bf16[1,4096,128]{2,1,0:T(8,128)(2,1)}, u32[]{:S(2)}) copy-start(bf16[1,4096,128]{2,1,0:T(8,128)(2,1)} %param.24) | copy-start | bytes 3145732
  109.2 2.0 copy-start.3
  109.2 158.0 %all-reduce.4.cloned.1.call-start = ((), (), s32[]{:S(2)}) async-start(), calls=%async_computation.3 | async-start | bytes 1179648 | tf_op jit(solution)/shard_map/psum | solution.py:102
  111.2 29.5 %copy-start.2 = (bf16[1,4,128,512]{3,2,1,0:T(8,128)(2,1)S(1)}, bf16[1,4,128,512]{3,2,1,0:T(8,128)(2,1)}, u32[]{:S(2)}) copy-start(bf16[1,4,128,512]{3,2,1,0:T(8,128)(2,1)} %param.17) | copy-start | bytes 1572868
  151.6 118.6 %all-to-all-start.2 = ((bf16[32,16,256]{2,1,0:T(8,128)(2,1)}), bf16[32,16,256]{2,1,0:T(8,128)(2,1)S(1)}, u32[]{:S(2)}, u32[]{:S(2)}) async-start(bf16[32,16,256]{2,1,0:T(8,128)(2,1)} %convolution_convert_fusion.1), calls=%async_computation.2 | async-start | bytes 524288 | tf_op jit(solution)/shard_map/all_to_all | solution.py:154
Sparse Core Ops, SparseCore 0:
  32.1 71.3 all-gather.2
  109.3 39.2 all-gather.4
  150.9 116.2 all-reduce.3
where the time goes:
time: 278 us
  waiting for transfers between devices  164 us (59%)
  blocking collectives  45.7 us (16%)
  starting transfers between devices  20.6 us (7%)
  matrix products  15 us (5%)
  between operations  14.7 us (5%)
  local copies, waits for them, and re-layouts  9.25 us (3%)
  other arithmetic  8.53 us (3%)
    psum x1, waiting for transfers between devices, on_device(): lax.psum(jnp.concatenate([part_blend.reshape(all_rows, HQ * HD), total_ro...  106 us
    all_gather x1, waiting for transfers between devices, on_device(): arrived = lax.all_gather(arrived_cols, 'kv', axis=1, tiled=True)  55.1 us
    pmax x1, blocking collectives, on_device(): highest = lax.pmax(part_high, 'kv')  24.3 us
    all_to_all x1, blocking collectives, on_device(): lax.all_to_all(outgoing, 'ep', split_axis=0, concat_axis=0, tiled=True)  21.4 us
    all_to_all x1, starting transfers between devices, on_device(): lax.all_to_all(down_split, 'kv', split_axis=1, concat_axis=0, tiled=True)  10.5 us
    all_to_all x1, starting transfers between devices, on_device(): lax.all_to_all(summed.reshape(ep_count, CAP, -1).astype(jnp.bfloat16), 'e...  9.89 us
  transfers between devices with their start and end apart: 5, of which 3 were waited for; matrix products, arithmetic and copies ran while one was open for 10% of the time, Pallas kernels for 0%

commit v1 on v0

--- a/solution.py
+++ b/solution.py
@@ -99,8 +99,11 @@
         preferred_element_type=jnp.float32,
     )
     total_row = jnp.pad(part_total.reshape(1, -1), ((0, 0), (0, HQ * HD - all_rows * HQ)))
-    packed = lax.psum(
-        jnp.concatenate([part_blend.reshape(all_rows, HQ * HD), total_row], axis=0), "kv"
+    packed = jnp.sum(
+        lax.all_gather(
+            jnp.concatenate([part_blend.reshape(all_rows, HQ * HD), total_row], axis=0), "kv"
+        ),
+        axis=0,
     )
     row_total = packed[all_rows, : all_rows * HQ].reshape(all_rows, HQ)
     blended = packed[:all_rows].reshape(all_rows, HQ, HD)

time: 278 us -> 220 us (0.79)
  the two profiles are of different devices: /device:TPU:2 before, /device:TPU:1 now
where the time goes in v1:
time: 220 us; the launch traced here: 219 us
  blocking collectives  103 us (47%)
  waiting for transfers between devices  68.5 us (31%)
  between operations  14.7 us (7%)
  matrix products  14.3 us (6%)
  other arithmetic  13 us (6%)
  local copies, waits for them, and re-layouts  5.28 us (2%)
    all_gather x1, waiting for transfers between devices, on_device(): arrived = lax.all_gather(arrived_cols, 'kv', axis=1, tiled=True)  52.2 us
    all_to_all x1, blocking collectives, on_device(): lax.all_to_all(down_split, 'kv', split_axis=1, concat_axis=0, tiled=True)  38.9 us
    pmax x1, blocking collectives, on_device(): highest = lax.pmax(part_high, 'kv')  23.6 us
    all_to_all x1, blocking collectives, on_device(): lax.all_to_all(summed.reshape(ep_count, CAP, -1).astype(jnp.bfloat16), 'e...  20.5 us
    all_to_all x1, blocking collectives, on_device(): lax.all_to_all(outgoing, 'ep', split_axis=0, concat_axis=0, tiled=True)  20.1 us
    all_gather x1, waiting for transfers between devices, on_device(): lax.all_gather(jnp.concatenate([part_blend.reshape(all_rows, HQ * HD), to...  16.3 us
    reduce_sum x1, other arithmetic, on_device(): jnp.sum(lax.all_gather(jnp.concatenate([part_blend.reshape(all_rows, HQ *...  4.44 us
  transfers between devices with their start and end apart: 3, of which 2 were waited for; matrix products, arithmetic and copies ran while one was open for 8% of the time, Pallas kernels for 0%

profile of v1, /device:TPU:1, one launch (start us, length us, event | category | flops | bytes accessed | tf_op | source)
XLA Modules:
  0.0 219.0 jit_solution(12370066087555320939)
XLA Ops:
  7.3 0.9 copy.46
  8.8 0.8 convert_reduce_fusion
  9.6 1.0 convolution_convert_fusion
  10.6 20.1 %all_to_all.25 = bf16[32,16,256]{2,1,0:T(8,128)(2,1)} all-to-all(bf16[32,16,256]{2,1,0:T(8,128)(2,1)S(1)} %bitcast.96), channel_id=1, replica_groups=mesh['kv'=16,'ep'=32] {'ep'}, dimensions={0} | all-to-all | bytes 524288 | tf_op jit(solution)/shard_map/all_to_all | solution.py:139
  31.4 1.0 convert_bitcast_fusion
  32.6 0.9 copy.41
  33.9 52.2 %all-gather.6.cloned.1.call-done = bf16[512,4096]{1,0:T(8,128)(2,1)} async-done(((bf16[512,256]{1,0:T(8,128)(2,1)}), bf16[512,4096]{1,0:T(8,128)(2,1)}) %all-gather.6.cloned.1.call-update) | async-done | bytes 4194320 | tf_op jit(solution)/shard_map/all_gather | solution.py:142
  86.1 3.6 %fusion.11 = f32[512,128]{1,0:T(8,128)S(1)} fusion(bf16[512,4096]{1,0:T(8,128)(2,1)} %all-gather.6.cloned.1.call-done, bf16[1,4096,128]{2,1,0:T(8,128)(2,1)S(1)} %copy-done), kind=kOutput, calls=%fused_computation.14 | convolution fusion | flops 536870912 | bytes 5505024 | tf_op jit(solution)/shard_map/dot_general | solution.py:143
  89.9 1.9 fusion.9
  92.0 0.7 bitcast_convert_fusion
  93.4 0.3 subtract_convert_fusion
  93.8 2.2 fusion
  96.0 23.6 %pmax.7 = f32[64,4,4]{0,2,1:T(4,128)S(1)} all-reduce(f32[64,4,4]{0,2,1:T(4,128)S(1)} %get-tuple-element.14), channel_id=1, replica_groups=mesh['kv'=16,'ep'=32] {'kv'}, use_global_device_ids=true, to_apply=%region_2.3 | all-reduce | flops 1024 | bytes 8192 | tf_op jit(solution)/shard_map/pmax | solution.py:92
  119.6 0.7 dynamic-slice_bitcast_fusion
  120.3 2.5 %fusion.6 = f32[64,4,4,128]{3,0,2,1:T(8,128)S(1)} fusion(f32[4,516,64,4]{1,2,3,0:T(8,128)} %get-tuple-element.15, f32[64,4,4]{0,2,1:T(4,128)S(1)} %pmax.7, pred[64,516]{1,0:T(8,128)(4,1)S(1)} %compare_and_fusion, bf16[4,4,128]{2,0,1:T(4,128)(2,1)S(1)} %dynamic-slice_bitcast_fusion, bf16[512,4,128]{2,0,1:T(8,128)(2,1)S(1)} %copy.40), kind=kOutput, calls=%fused_computation.7 | convolution fusion | flops 138964992 | bytes 3203328 | tf_op jit(solution)/shard_map/nkgm,mkd->nkgd/dot_general | solution.py:95
  123.4 2.7 %fusion.1 = f32[64,4,4]{0,2,1:T(4,128)S(1)} fusion(f32[4,516,64,4]{1,2,3,0:T(8,128)} %get-tuple-element.15, f32[64,4,4]{0,2,1:T(4,128)S(1)} %pmax.7, pred[64,516]{1,0:T(8,128)(4,1)S(1)} %compare_and_fusion), kind=kLoop, calls=%fused_computation.3 | loop fusion | flops 2640896 | bytes 2154752 | tf_op jit(solution)/shard_map/reduce_sum | solution.py:94
  126.5 0.9 fusion.13
  128.0 38.9 %all_to_all.26 = bf16[128,16,256]{2,0,1:T(8,128)(2,1)S(1)} all-to-all(bf16[128,16,256]{2,0,1:T(8,128)(2,1)S(1)} %copy.48), channel_id=1, replica_groups=mesh['kv'=16,'ep'=32] {'kv'}, dimensions={1} | all-to-all | bytes 2097152 | tf_op jit(solution)/shard_map/all_to_all | solution.py:148
  166.8 2.4 %convolution_convert_fusion.1 = bf16[32,16,256]{2,1,0:T(8,128)(2,1)S(1)} fusion(bf16[32,16,2048]{2,1,0:T(8,128)(2,1)} %bitcast.99, bf16[2048,256,1]{1,0,2:T(8,128)(2,1)S(1)} %bitcast.93), kind=kOutput, calls=%fused_computation.9 | convolution fusion | flops 537001984 | bytes 3407872 | tf_op jit(solution)/shard_map/dot_general | solution.py:151
  169.2 20.5 %all_to_all.27 = bf16[32,16,256]{2,1,0:T(8,128)(2,1)S(1)} all-to-all(bf16[32,16,256]{2,1,0:T(8,128)(2,1)S(1)} %convolution_convert_fusion.1), channel_id=1, replica_groups=mesh['kv'=16,'ep'=32] {'ep'}, dimensions={0} | all-to-all | bytes 524288 | tf_op jit(solution)/shard_map/all_to_all | solution.py:157
  189.7 0.9 convolution_convert_fusion.2
  190.6 16.3 %all-gather.10.cloned.1.call-done = f32[16,65,2048]{2,1,0:T(8,128)} async-done(((f32[1,65,2048]{2,1,0:T(8,128)}), f32[16,65,2048]{2,1,0:T(8,128)}) %all-gather.10.cloned.1.call-update) | async-done | bytes 8519696 | tf_op jit(solution)/shard_map/all_gather | solution.py:103
  206.8 4.4 %reduce_sum.56 = f32[65,2048]{1,0:T(8,128)S(1)} reduce(f32[16,65,2048]{2,1,0:T(8,128)} %all-gather.10.cloned.1.call-done, f32[]{:T(128)} %constant.75.clone.1), dimensions={0}, to_apply=%region_4.5 | reduce | flops 1996800 | bytes 9052164 | tf_op jit(solution)/shard_map/reduce_sum | solution.py:102
  211.6 0.9 fusion.25
  (58 shorter events, 4.2 us)
Async XLA Ops:
  7.2 78.9 %copy-start = (bf16[1,4096,128]{2,1,0:T(8,128)(2,1)S(1)}, bf16[1,4096,128]{2,1,0:T(8,128)(2,1)}, u32[]{:S(2)}) copy-start(bf16[1,4096,128]{2,1,0:T(8,128)(2,1)} %param.23) | copy-start | bytes 3145732
  7.2 25.3 %copy-start.3 = (bf16[1,4,128,512]{3,2,1,0:T(8,128)(2,1)S(1)}, bf16[1,4,128,512]{3,2,1,0:T(8,128)(2,1)}, u32[]{:S(2)}) copy-start(bf16[1,4,128,512]{3,2,1,0:T(8,128)(2,1)} %param.16) | copy-start | bytes 1572868
  7.2 78.9 %all-gather.6.cloned.1.call-start = ((), (), s32[]{:S(2)}) async-start(), calls=%async_computation.3 | async-start | bytes 4456448 | tf_op jit(solution)/shard_map/all_gather | solution.py:142
  8.4 25.1 %copy-start.4 = (bf16[1,4,128,512]{3,2,1,0:T(8,128)(2,1)S(1)}, bf16[1,4,128,512]{3,2,1,0:T(8,128)(2,1)}, u32[]{:S(2)}) copy-start(bf16[1,4,128,512]{3,2,1,0:T(8,128)(2,1)} %param.17) | copy-start | bytes 1572868
  30.7 136.1 %all-gather.8.cloned.1.call-start = ((), (), s32[]{:S(2)}) async-start(), calls=%async_computation.4 | async-start | bytes 2228224 | tf_op jit(solution)/shard_map/all_gather | solution.py:152
  32.4 1.3 copy-start.7
  86.1 3.6 %copy-start.1 = (bf16[512,4096]{1,0:T(8,128)(2,1)S(1)}, bf16[512,4096]{1,0:T(8,128)(2,1)}, u32[]{:S(2)}) copy-start(bf16[512,4096]{1,0:T(8,128)(2,1)} %all-gather.6.cloned.1.call-done) | copy-start | bytes 12582916
  86.1 3.7 %copy-start.6 = (bf16[1,4096,128]{2,1,0:T(8,128)(2,1)S(1)}, bf16[1,4096,128]{2,1,0:T(8,128)(2,1)}, u32[]{:S(2)}) copy-start(bf16[1,4096,128]{2,1,0:T(8,128)(2,1)} %param.24) | copy-start | bytes 3145732
  91.8 2.0 copy-start.5
  91.8 115.0 %all-gather.10.cloned.1.call-start = ((), (), s32[]{:S(2)}) async-start(), calls=%async_computation.5 | async-start | bytes 10027008 | tf_op jit(solution)/shard_map/all_gather | solution.py:103
  123.2 4.2 %copy-start.2 = (bf16[1,128,4096]{2,1,0:T(8,128)(2,1)S(1)}, bf16[1,128,4096]{2,1,0:T(8,128)(2,1)}, u32[]{:S(2)}) copy-start(bf16[1,128,4096]{2,1,0:T(8,128)(2,1)} %param.25) | copy-start | bytes 3145732
Sparse Core Ops, SparseCore 0:
  30.8 55.2 all-gather.5
  91.9 41.9 all-gather.7
  136.0 70.7 all-gather.9
